TPU v7x, 32 devices: a whole 2x2x4 slice. The times are simulated.
32 devices in a mesh: ctx: 8 (over z, x), probe: 4 (over y, core).
Axes of the slice: x: 2, y: 2, z: 4, core: 2. Of those that a mesh axis runs over, the one named last changes fastest.
Arguments:
- features: float32 [3, 2048, 1024], P(None, 'ctx'), may hold values from -6 to 6
- cotangent: float32 [2048, 1024], P('ctx'), may hold values from -48 to 48
- gate_logits: float32 [4], replicated, may hold values from -4 to 4
- probes: int32 [4, 3, 2048, 1024], P('probe', None, 'ctx'), may hold values from -1 to 1, as said below
Outputs:
- products: float32 [4, 3, 2048, 1024], P('probe', None, 'ctx')
- block_trace: float32 [8, 3, 4], P('ctx')
Inputs may be any that keep to these rules, and one draw needn't show every extreme that they name: `probes`: every entry is -1 or 1.
All inputs are finite; a program needn't handle non-finite values.
Results may differ from a plain program's by a relative error of at most 0.0003.
Values sent between devices are 32-bit elements; how exact they have to be, the bound alone decides.
No kernel may reach another device: no remote copies, remote signals or barrier semaphores. Data moves between devices by JAX's collectives and lax.ppermute only.
A program may use at most 192 MiB of HBM per device.

v0:
```python
import jax
import jax.numpy as jnp
from jax import lax
from jax.sharding import PartitionSpec as P

HIGHEST = lax.Precision.HIGHEST


def entering(part, axis, combine, identity, reverse):
    count = lax.axis_size(axis)
    place = lax.axis_index(axis)
    ahead = count - 1 - place if reverse else place
    gathered = jax.tree.map(lambda a: lax.all_gather(a, axis), part)
    state = jax.tree.map(lambda a, e: jnp.zeros_like(a) + jnp.asarray(e, a.dtype), part, identity)

    def one(turn, state):
        source = count - 1 - turn if reverse else turn
        return combine(
            state, jax.tree.map(lambda a: lax.dynamic_index_in_dim(a, source, 0, False), gathered)
        )

    return lax.fori_loop(0, ahead, one, state)


def feature_map(inputs):
    return jnp.where(inputs > 0, inputs + 1.0, jnp.exp(jnp.minimum(inputs, 0.0)))


def feature_slope(inputs):
    return jnp.where(inputs > 0, 1.0, jnp.exp(jnp.minimum(inputs, 0.0)))


def feature_curve(inputs):
    return jnp.where(inputs > 0, 0.0, jnp.exp(jnp.minimum(inputs, 0.0)))


def segment_loss(query_rows, key_rows, value_rows, memory, normalizer, cot_rows, gate_logits):
    query_feat = feature_map(query_rows)
    retrieved = jnp.einsum("sha,hab->shb", query_feat, memory, precision=HIGHEST)
    denom_mem = jnp.einsum("sha,ha->sh", query_feat, normalizer, precision=HIGHEST) + 1.0
    from_memory = retrieved / denom_mem[:, :, None]
    seg_rows = query_rows.shape[0]
    scale = query_rows.shape[-1] ** (-0.5)
    causal = lax.broadcasted_iota(jnp.int32, (seg_rows, seg_rows), 0) >= lax.broadcasted_iota(
        jnp.int32, (seg_rows, seg_rows), 1
    )
    logits = jnp.einsum("sha,tha->hst", query_rows, key_rows, precision=HIGHEST) * scale
    logits = jnp.where(causal[None], logits, -1e30)
    top = lax.stop_gradient(jnp.max(logits, axis=2, keepdims=True))
    weights = jnp.exp(logits - top)
    local_num = jnp.einsum("hst,thb->shb", weights, value_rows, precision=HIGHEST)
    local_den = jnp.transpose(jnp.sum(weights, axis=2))
    from_local = local_num / local_den[:, :, None]
    mixing = jax.nn.sigmoid(gate_logits)[None, :, None]
    output = mixing * from_memory + (1.0 - mixing) * from_local
    return jnp.sum(cot_rows * output)


def add_trees(earlier, later):
    return jax.tree.map(jnp.add, earlier, later)


def shards(features, cotangent, gate_logits, probes):
    heads = gate_logits.shape[0]
    seg_rows = features.shape[1]
    head_size = features.shape[2] // heads
    shaped = features.reshape(3, seg_rows, heads, head_size)
    query_rows, key_rows, value_rows = (shaped[0], shaped[1], shaped[2])
    cot_rows = cotangent.reshape(seg_rows, heads, head_size)
    signs = probes[0].astype(jnp.float32).reshape(3, seg_rows, heads, head_size)
    query_dir, key_dir, value_dir = (signs[0], signs[1], signs[2])
    key_feat = feature_map(key_rows)
    key_slope = feature_slope(key_rows)
    key_tan = key_slope * key_dir
    increment = jnp.einsum("sha,shb->hab", key_feat, value_rows, precision=HIGHEST)
    norm_inc = jnp.sum(key_feat, axis=0)
    increment_tan = jnp.einsum("sha,shb->hab", key_tan, value_rows, precision=HIGHEST) + jnp.einsum(
        "sha,shb->hab", key_feat, value_dir, precision=HIGHEST
    )
    norm_tan = jnp.sum(key_tan, axis=0)
    groups = lax.axis_size("probe")
    share = heads // groups
    first_head = lax.axis_index("probe") * share
    zero_mem = jnp.zeros((heads, head_size, head_size), jnp.float32)
    zero_norm = jnp.zeros((heads, head_size), jnp.float32)
    zero_share = jnp.zeros((share, head_size, head_size), jnp.float32)
    own_inc = lax.dynamic_slice_in_dim(increment, first_head, share, 0)
    own_prefix, normalizer, memory_tan, normalizer_tan = entering(
        (own_inc, norm_inc, increment_tan, norm_tan),
        "ctx",
        add_trees,
        (zero_share, zero_norm, zero_mem, zero_norm),
        False,
    )
    memory = lax.all_gather(own_prefix, "probe", axis=0, tiled=True)

    def local_loss(point):
        return segment_loss(point[0], point[1], point[2], point[3], point[4], cot_rows, gate_logits)

    point = (query_rows, key_rows, value_rows, memory, normalizer)
    grads, pullback = jax.vjp(jax.grad(local_loss), point)
    curvature = pullback((query_dir, key_dir, value_dir, memory_tan, normalizer_tan))[0]
    own_back = lax.dynamic_slice_in_dim(grads[3], first_head, share, 0)
    own_suffix, back_norm, back_mem_tan, back_norm_tan = entering(
        (own_back, grads[4], curvature[3], curvature[4]),
        "ctx",
        add_trees,
        (zero_share, zero_norm, zero_mem, zero_norm),
        True,
    )
    back_mem = lax.all_gather(own_suffix, "probe", axis=0, tiled=True)
    through = jnp.einsum("shb,hab->sha", value_rows, back_mem, precision=HIGHEST) + back_norm[None]
    through_tan = (
        jnp.einsum("shb,hab->sha", value_dir, back_mem, precision=HIGHEST)
        + jnp.einsum("shb,hab->sha", value_rows, back_mem_tan, precision=HIGHEST)
        + back_norm_tan[None]
    )
    key_out = curvature[1] + feature_curve(key_rows) * key_dir * through + key_slope * through_tan
    value_out = (
        curvature[2]
        + jnp.einsum("sha,hab->shb", key_tan, back_mem, precision=HIGHEST)
        + jnp.einsum("sha,hab->shb", key_feat, back_mem_tan, precision=HIGHEST)
    )
    stacked = jnp.stack((curvature[0], key_out, value_out))
    products = stacked.reshape(1, 3, seg_rows, heads * head_size)
    partial_trace = jnp.sum(signs * stacked, axis=(1, 3)) / (seg_rows * groups)
    block_trace = lax.psum(partial_trace, "probe")
    return (products, block_trace.reshape(1, 3, heads))


def solution(mesh):
    placed = (P(None, "ctx", None), P("ctx", None), P(), P("probe", None, "ctx", None))
    return jax.shard_map(
        shards,
        mesh=mesh,
        in_specs=placed,
        out_specs=(P("probe", None, "ctx", None), P("ctx", None, None)),
        check_vma=False,
    )
```

profile of v0, /device:TPU:0, one launch (start us, length us, event | category | flops | bytes accessed | tf_op | source)
XLA Modules:
  0.0 484.1 jit_solution(11972801363494513276)
XLA Ops:
  7.2 3.1 fusion.134
  13.2 3.5 copy.177
  16.8 2.1 convert_element_type.6
  22.3 2.4 convolution_add_fusion.7
  24.8 1.7 fusion.52
  28.1 2.6 copy.179
  30.6 32.7 %all_gather.57 = f32[8,4,256]{2,1,0:T(4,128)S(1)} all-gather(f32[1,4,256]{2,1,0:T(4,128)S(1)} %all_gather.56), channel_id=1, replica_groups=mesh['ctx'=8,'probe'=4] {'ctx'}, dimensions={0}, use_global_device_ids=true | all-gather | bytes 36864 | tf_op jit(solution)/shard_map/all_gather | solution.py:13
  63.3 31.3 %all_gather.61 = f32[8,4,256]{2,1,0:T(4,128)S(1)} all-gather(f32[1,4,256]{2,1,0:T(4,128)S(1)} %all_gather.60), channel_id=1, replica_groups=mesh['ctx'=8,'probe'=4] {'ctx'}, dimensions={0}, use_global_device_ids=true | all-gather | bytes 36864 | tf_op jit(solution)/shard_map/all_gather | solution.py:13
  94.6 1.9 fusion.23
  97.1 1.9 fusion.55
  99.0 3.0 multiply_reduce_fusion.5
  104.0 87.6 %all-gather.21.cloned.1.call-done = f32[32,256,256]{2,1,0:T(8,128)} async-done(((f32[4,256,256]{2,1,0:T(8,128)}), f32[32,256,256]{2,1,0:T(8,128)}) %all-gather.21.cloned.1.call-update) | async-done | bytes 8388624 | tf_op jit(solution)/shard_map/all_gather | solution.py:13
  196.2 1.9 fusion.44
  198.9 2.9 fusion.132
  201.8 23.2 %all-gather.15.cloned.1.call-done = f32[4,256,256]{2,1,0:T(8,128)} async-done(((f32[1,256,256]{2,1,0:T(8,128)}), f32[4,256,256]{2,1,0:T(8,128)}) %all-gather.15.cloned.1.call-update) | async-done | bytes 1048592 | tf_op jit(solution)/shard_map/all_gather | solution.py:95
  225.1 3.3 convolution_bitcast_fusion.5
  228.5 1.7 multiply_reduce_fusion.3
  230.3 2.0 fusion.36
  234.8 2.5 fusion.42
  237.3 2.6 convolution_add_fusion.2
  240.0 2.8 fusion.135
  245.5 2.3 fusion.2
  251.0 30.9 %all-gather.7 = f32[8,4,256]{2,1,0:T(4,128)S(1)} all-gather(f32[1,4,256]{2,1,0:T(4,128)S(1)} %fusion.102), channel_id=7, replica_groups=mesh['ctx'=8,'probe'=4] {'ctx'}, dimensions={0}, use_global_device_ids=true | all-gather | bytes 36864 | tf_op jit(solution)/shard_map/all_gather | solution.py:13
  281.9 31.1 %all-gather.6 = f32[8,4,256]{2,1,0:T(4,128)S(1)} all-gather(f32[1,4,256]{2,1,0:T(4,128)S(1)} %bitcast.357), channel_id=5, replica_groups=mesh['ctx'=8,'probe'=4] {'ctx'}, dimensions={0}, use_global_device_ids=true | all-gather | bytes 36864 | tf_op jit(solution)/shard_map/all_gather | solution.py:13
  313.0 2.1 convolution_add_fusion.13
  315.1 2.4 fusion.15
  317.5 2.3 fusion.90
  319.8 2.3 fusion.89
  322.2 3.1 fusion.21
  325.3 84.8 %all-gather.25.cloned.1.call-done = f32[32,256,256]{2,1,0:T(8,128)} async-done(((f32[4,256,256]{2,1,0:T(8,128)}), f32[32,256,256]{2,1,0:T(8,128)}) %all-gather.25.cloned.1.call-update) | async-done | bytes 8388624 | tf_op jit(solution)/shard_map/all_gather | solution.py:13
  411.2 26.5 %while.35 = (s32[]{:T(128)}, f32[1,256,256]{2,1,0:T(8,128)S(1)}, f32[4,256]{1,0:T(4,128)S(1)}, f32[4,256,256]{2,1,0:T(8,128)}, f32[4,256]{1,0:T(4,128)S(1)}, /*i...) while((s32[]{:T(128)}, f32[1,256,256]{2,1,0:T(8,128)S(1)}, ...), condition=%wide.region_14.15_spmd, body=%wide.region_13.14_spmd.sunk | while | flops 329734 | bytes 3956927 | solution.py:22
  411.2 2.7 bitcast_add_fusion.22
  415.0 2.7 bitcast_add_fusion.22
  418.7 2.7 bitcast_add_fusion.22
  422.4 2.7 bitcast_add_fusion.22
  426.1 2.7 bitcast_add_fusion.22
  429.9 2.7 bitcast_add_fusion.22
  433.6 2.7 bitcast_add_fusion.22
  438.5 3.1 fusion.11
  441.7 2.2 fusion.27
  443.9 1.9 fusion.35
  445.9 2.3 fusion.28
  448.2 4.3 all-gather.17.cloned.1.call-done
  452.6 3.8 fusion.1
  456.4 1.9 fusion
  464.9 2.1 multiply_reduce_fusion
  467.1 3.5 copy.216
  470.6 5.9 %psum.7 = f32[1,3,4]{2,1,0:T(4,128)S(1)} all-reduce(f32[1,3,4]{2,1,0:T(4,128)S(1)} %multiply_bitcast_fusion), channel_id=1, replica_groups=mesh['ctx'=8,'probe'=4] {'probe'}, use_global_device_ids=true, to_apply=%region_17.18 | all-reduce | flops 12 | bytes 96 | tf_op jit(solution)/shard_map/psum | solution.py:127
  (187 shorter events, 40.4 us)
Async XLA Ops:
  7.2 96.9 %all-gather.19.cloned.1.call-start = ((), (), s32[]{:S(2)}) async-start(), calls=%async_computation.2 | async-start | bytes 2359296 | tf_op jit(solution)/shard_map/all_gather | solution.py:13
  11.0 9.9 %copy-start.8 = (f32[1,256,1024]{1,2,0:T(8,128)}, f32[1,256,1024]{1,2,0:T(8,128)S(1)}, u32[]{:S(2)}) copy-start(f32[1,256,1024]{1,2,0:T(8,128)S(1)} %copy.172) | copy-start | bytes 3145732
  13.2 178.5 %all-gather.21.cloned.1.call-start = ((), (), s32[]{:S(2)}) async-start(), calls=%async_computation.3 | async-start | bytes 9437184 | tf_op jit(solution)/shard_map/all_gather | solution.py:13
  18.9 2.0 copy-start.20
  20.9 78.1 %copy-start.13 = (f32[1,1,256,1024]{2,3,1,0:T(8,128)}, f32[1,1,256,1024]{2,3,1,0:T(8,128)S(1)}, u32[]{:S(2)}) copy-start(f32[1,1,256,1024]{2,3,1,0:T(8,128)S(1)} %get-tuple-element.345) | copy-start | bytes 3145732
  24.7 200.3 %all-gather.15.cloned.1.call-start = ((), (), s32[]{:S(2)}) async-start(), calls=%async_computation | async-start | bytes 1310720 | tf_op jit(solution)/shard_map/all_gather | solution.py:95
  30.6 66.5 %copy-start.36 = (f32[256,4,256]{2,0,1:T(8,128)S(1)}, f32[256,4,256]{2,0,1:T(8,128)}, u32[]{:S(2)}) copy-start(f32[256,4,256]{2,0,1:T(8,128)} %copy.179) | copy-start | bytes 3145732
  97.1 4.9 %copy-start.1 = (f32[4,256,256]{1,2,0:T(8,128)}, f32[4,256,256]{1,2,0:T(8,128)S(1)}, u32[]{:S(2)}) copy-start(f32[4,256,256]{1,2,0:T(8,128)S(1)} %subtract_exponential_fusion) | copy-start | bytes 3145732
  99.0 3.6 copy-start.23
  102.0 143.5 %copy-start.40 = (f32[256,4]{0,1:T(4,128)}, f32[256,4]{0,1:T(4,128)S(1)}, u32[]{:S(2)}) copy-start(f32[256,4]{0,1:T(4,128)S(1)} %multiply_divide_fusion.3) | copy-start | bytes 12292
  192.5 132.7 %all-gather.23.cloned.1.call-start = ((), (), s32[]{:S(2)}) async-start(), calls=%async_computation.4 | async-start | bytes 2359296 | tf_op jit(solution)/shard_map/all_gather | solution.py:13
  193.8 121.3 %copy-start.49 = (f32[4]{0:T(128)}, f32[4]{0:T(128)S(1)}, u32[]{:S(2)}) copy-start(f32[4]{0:T(128)S(1)} %get-tuple-element.336) | copy-start | bytes 52
  193.8 128.4 %copy-start.47 = (f32[4]{0:T(128)}, f32[4]{0:T(128)S(1)}, u32[]{:S(2)}) copy-start(f32[4]{0:T(128)S(1)} %get-tuple-element.335) | copy-start | bytes 52
  195.4 3.5 copy-start.6
  196.2 41.1 %copy-start.42 = (f32[256,4]{0,1:T(4,128)}, f32[256,4]{0,1:T(4,128)S(1)}, u32[]{:S(2)}) copy-start(f32[256,4]{0,1:T(4,128)S(1)} %multiply_divide_fusion.2) | copy-start | bytes 12292
  198.9 38.4 %copy-start.44 = (f32[256,4]{0,1:T(4,128)}, f32[256,4]{0,1:T(4,128)S(1)}, u32[]{:S(2)}) copy-start(f32[256,4]{0,1:T(4,128)S(1)} %fusion.104) | copy-start | bytes 12292
  198.9 29.5 %copy-start.45 = (f32[256,4]{0,1:T(4,128)S(1)}, f32[256,4]{0,1:T(4,128)}, u32[]{:S(2)}) copy-start(f32[256,4]{0,1:T(4,128)} %negate_bitcast_fusion) | copy-start | bytes 12292
  225.1 3.4 copy-start.2
  225.1 3.4 copy-start.9
  232.3 82.8 %copy-start.51 = (f32[256,4]{0,1:T(4,128)}, f32[256,4]{0,1:T(4,128)S(1)}, u32[]{:S(2)}) copy-start(f32[256,4]{0,1:T(4,128)S(1)} %get-tuple-element.352) | copy-start | bytes 12292
  234.6 175.5 %all-gather.25.cloned.1.call-start = ((), (), s32[]{:S(2)}) async-start(), calls=%async_computation.5 | async-start | bytes 9437184 | tf_op jit(solution)/shard_map/all_gather | solution.py:13
  239.9 212.7 %all-gather.17.cloned.1.call-start = ((), (), s32[]{:S(2)}) async-start(), calls=%async_computation.1 | async-start | bytes 1310720 | tf_op jit(solution)/shard_map/all_gather | solution.py:111
  240.0 2.9 copy-start.3
  240.0 2.9 copy-start.10
  240.0 2.9 copy-start.33
  245.5 3.4 copy-start.22
  247.8 67.3 %copy-start.53 = (f32[4,256]{1,0:T(4,128)}, f32[4,256]{1,0:T(4,128)S(1)}, u32[]{:S(2)}) copy-start(f32[4,256]{1,0:T(4,128)S(1)} %get-tuple-element.349) | copy-start | bytes 12292
  249.9 65.2 %copy-start.7 = (f32[4,256,256]{2,1,0:T(8,128)S(1)}, f32[4,256,256]{2,1,0:T(8,128)}, u32[]{:S(2)}) copy-start(f32[4,256,256]{2,1,0:T(8,128)} %copy-done.5) | copy-start | bytes 3145732
  315.1 2.4 copy-start.14
  317.5 2.3 copy-start.24
  319.8 2.3 copy-start.18
  411.2 27.3 %copy-start.43 = (f32[256,4]{0,1:T(4,128)S(1)}, f32[256,4]{0,1:T(4,128)}, u32[]{:S(2)}) copy-start(f32[256,4]{0,1:T(4,128)} %copy-done.42) | copy-start | bytes 12292
  437.7 3.9 copy-start.41
  437.7 3.9 copy-start.46
  437.7 3.9 copy-start.48
  438.5 3.1 copy-start.4
  438.5 3.1 copy-start.11
  438.5 3.1 copy-start.39
  441.6 2.2 copy-start.25
  441.6 2.2 copy-start.29
  441.6 2.2 copy-start.50
  441.7 2.2 copy-start.52
  441.7 2.2 copy-start.54
  448.2 8.2 %copy-start = (f32[4,256,256]{2,1,0:T(8,128)S(1)}, f32[4,256,256]{2,1,0:T(8,128)}, u32[]{:S(2)}) copy-start(f32[4,256,256]{2,1,0:T(8,128)} %get-tuple-element.195) | copy-start | bytes 3145732
  456.4 2.0 copy-start.19
  456.4 2.0 copy-start.30
  456.4 3.1 copy-start.12
  462.7 2.2 copy-start.34
  (13 other events, 19.8 us)
Sparse Core Ops, SparseCore 0:
  13.3 52.4 all-gather.18
  67.9 123.7 all-gather.20
  193.2 31.8 all-gather.14
  234.7 49.8 all-gather.22
  286.5 123.4 all-gather.24
  438.6 13.9 all-gather.16
where the time goes:
time: 491 us; the launch traced here: 484 us
  waiting for transfers between devices  200 us (41%)
  blocking collectives  132 us (27%)
  matrix products  75.6 us (15%)
  other arithmetic  35.3 us (7%)
  local copies, waits for them, and re-layouts  24.5 us (5%)
  between operations  15.3 us (3%)
    all_gather x4, waiting for transfers between devices, entering(): gathered = jax.tree.map(lambda a: lax.all_gather(a, axis), part)  172 us
    all_gather x4, blocking collectives, entering(): gathered = jax.tree.map(lambda a: lax.all_gather(a, axis), part)  126 us
    add x21, other arithmetic, add_trees(): return jax.tree.map(jnp.add, earlier, later)  25.9 us
    all_gather x1, waiting for transfers between devices, shards(): memory = lax.all_gather(own_prefix, 'probe', axis=0, tiled=True)  23.2 us
    dot_general x9, matrix products, segment_loss(): jnp.einsum('sha,hab->shb', query_feat, memory, precision=HIGHEST)  22.2 us
    dot_general x8, matrix products, segment_loss(): jnp.einsum('hst,thb->shb', weights, value_rows, precision=HIGHEST)  16.8 us
    dot_general x7, matrix products, segment_loss(): jnp.einsum('sha,tha->hst', query_rows, key_rows, precision=HIGHEST) * scale  15 us
    unnamed x116, local copies, waits for them, and re-layouts  14.3 us
  transfers between devices with their start and end apart: 6, of which 4 were waited for; matrix products, arithmetic and copies ran while one was open for 15% of the time, Pallas kernels for 0%

commit v1 on v0

--- a/solution.py
+++ b/solution.py
@@ -4,6 +4,19 @@
 from jax.sharding import PartitionSpec as P
 
 HIGHEST = lax.Precision.HIGHEST
+
+
+def ring_gather(x, axis, dim):
+    ways = lax.axis_size(axis)
+    up = [(d, (d + 1) % ways) for d in range(ways)]
+    down = [(d, (d - 1) % ways) for d in range(ways)]
+    earlier, later = ([x], [x])
+    for _ in range(ways // 2):
+        earlier.append(lax.ppermute(earlier[-1], axis, up))
+    for _ in range((ways - 1) // 2):
+        later.append(lax.ppermute(later[-1], axis, down))
+    line = jnp.concatenate([*earlier[::-1], *later[1:]], axis=dim)
+    return jnp.roll(line, (lax.axis_index(axis) - ways // 2) * x.shape[dim], axis=dim)
 
 
 def entering(part, axis, combine, identity, reverse):
@@ -92,7 +105,7 @@
         (zero_share, zero_norm, zero_mem, zero_norm),
         False,
     )
-    memory = lax.all_gather(own_prefix, "probe", axis=0, tiled=True)
+    memory = ring_gather(own_prefix, "probe", 0)
 
     def local_loss(point):
         return segment_loss(point[0], point[1], point[2], point[3], point[4], cot_rows, gate_logits)

time: 491 us -> 495 us (level)
  blocking collectives: 132 us -> 154 us
  waiting for transfers between devices: 200 us -> 179 us
    all_gather x1 -> x0, waiting for transfers between devices: 23.2 us -> none  [shards(): memory = lax.all_gather(own_prefix, 'probe', axis=0, tiled=True)]
    all_gather x4, blocking collectives: 126 us -> 148 us  [entering(): gathered = jax.tree.map(lambda a: lax.all_gather(a, axis), part)]
    ppermute x0 -> x3, waiting for transfers between devices: none -> 5.74 us  [the longest x2 5.74 us: ring_gather(): earlier.append(lax.ppermute(earlier[-1], axis, up))]
    unnamed x116 -> x135, local copies, waits for them, and re-layouts: 14.3 us -> 15.4 us
  transfers between devices with their start and end apart: 6 -> 8, of which waited for: 4 -> 4; matrix products, arithmetic and copies ran while one was open for 15% -> 15% of each run, Pallas kernels for 0% -> 0%
where the time goes in v1:
time: 495 us; the launch traced here: 488 us
  waiting for transfers between devices  179 us (36%)
  blocking collectives  154 us (31%)
  matrix products  75.2 us (15%)
  other arithmetic  35.7 us (7%)
  local copies, waits for them, and re-layouts  26.2 us (5%)
  between operations  15.3 us (3%)
    all_gather x4, waiting for transfers between devices, entering(): gathered = jax.tree.map(lambda a: lax.all_gather(a, axis), part)  173 us
    all_gather x4, blocking collectives, entering(): gathered = jax.tree.map(lambda a: lax.all_gather(a, axis), part)  148 us
    add x21, other arithmetic, add_trees(): return jax.tree.map(jnp.add, earlier, later)  25.8 us
    dot_general x9, matrix products, segment_loss(): jnp.einsum('sha,hab->shb', query_feat, memory, precision=HIGHEST)  22.7 us
    dot_general x8, matrix products, segment_loss(): jnp.einsum('hst,thb->shb', weights, value_rows, precision=HIGHEST)  17 us
    unnamed x135, local copies, waits for them, and re-layouts  15.4 us
    dot_general x7, matrix products, segment_loss(): jnp.einsum('sha,tha->hst', query_rows, key_rows, precision=HIGHEST) * scale  14 us
  transfers between devices with their start and end apart: 8, of which 4 were waited for; matrix products, arithmetic and copies ran while one was open for 15% of the time, Pallas kernels for 0%

profile of v1, /device:TPU:0, one launch (start us, length us, event | category | flops | bytes accessed | tf_op | source)
XLA Modules:
  0.0 488.0 jit_solution(14984807898409578619)
XLA Ops:
  7.2 3.1 fusion.141
  13.2 3.5 copy.187
  16.8 2.1 convert_element_type.6
  22.3 2.4 convolution_add_fusion.7
  24.8 1.8 fusion.51
  26.6 1.6 copy.283
  29.5 1.6 copy.177
  31.1 32.7 %all_gather.54 = f32[8,4,256]{2,1,0:T(4,128)S(1)} all-gather(f32[1,4,256]{2,1,0:T(4,128)S(1)} %all_gather.53), channel_id=1, replica_groups=mesh['ctx'=8,'probe'=4] {'ctx'}, dimensions={0}, use_global_device_ids=true | all-gather | bytes 36864 | tf_op jit(solution)/shard_map/all_gather | solution.py:26
  63.7 31.0 %all_gather.58 = f32[8,4,256]{2,1,0:T(4,128)S(1)} all-gather(f32[1,4,256]{2,1,0:T(4,128)S(1)} %all_gather.57), channel_id=1, replica_groups=mesh['ctx'=8,'probe'=4] {'ctx'}, dimensions={0}, use_global_device_ids=true | all-gather | bytes 36864 | tf_op jit(solution)/shard_map/all_gather | solution.py:26
  95.4 1.9 fusion.22
  97.9 1.9 fusion.54
  99.8 3.0 multiply_reduce_fusion.5
  105.4 2.1 convolution_bitcast_fusion.6
  107.6 83.8 %all-gather.18.cloned.1.call-done = f32[32,256,256]{2,1,0:T(8,128)} async-done(((f32[4,256,256]{2,1,0:T(8,128)}), f32[32,256,256]{2,1,0:T(8,128)}) %all-gather.18.cloned.1.call-update) | async-done | bytes 8388624 | tf_op jit(solution)/shard_map/all_gather | solution.py:26
  193.3 2.1 collective-permute-start.2
  195.5 2.1 fusion.117
  197.6 3.2 fusion.139
  202.3 5.7 %collective-permute-done.1 = f32[1,256,256]{1,2,0:T(8,128)S(1)} collective-permute-done((f32[1,256,256]{1,2,0:T(8,128)S(1)}, f32[1,256,256]{1,2,0:T(8,128)S(1)}, u32[]{:S(2)}, u32[]{:S(2)}) %collective-permute-start.1) | collective-permute-done | bytes 262176 | tf_op jit(solution)/shard_map/ppermute | solution.py:15
  210.3 1.8 multiply_reduce_fusion.3
  212.1 1.5 fusion.47
  214.5 2.6 fusion.41
  217.1 2.6 convolution_add_fusion.2
  219.9 2.5 fusion.142
  225.2 2.3 fusion.2
  230.7 53.4 %all-gather.7 = f32[8,4,256]{2,1,0:T(4,128)S(1)} all-gather(f32[1,4,256]{2,1,0:T(4,128)S(1)} %fusion.105), channel_id=7, replica_groups=mesh['ctx'=8,'probe'=4] {'ctx'}, dimensions={0}, use_global_device_ids=true | all-gather | bytes 36864 | tf_op jit(solution)/shard_map/all_gather | solution.py:26
  284.1 30.7 %all-gather.6 = f32[8,4,256]{2,1,0:T(4,128)S(1)} all-gather(f32[1,4,256]{2,1,0:T(4,128)S(1)} %bitcast.350), channel_id=5, replica_groups=mesh['ctx'=8,'probe'=4] {'ctx'}, dimensions={0}, use_global_device_ids=true | all-gather | bytes 36864 | tf_op jit(solution)/shard_map/all_gather | solution.py:26
  314.8 2.1 convolution_add_fusion.13
  316.9 2.4 fusion.15
  319.3 2.4 fusion.93
  321.7 3.1 fusion.20
  324.8 89.1 %all-gather.22.cloned.1.call-done = f32[32,256,256]{2,1,0:T(8,128)} async-done(((f32[4,256,256]{2,1,0:T(8,128)}), f32[32,256,256]{2,1,0:T(8,128)}) %all-gather.22.cloned.1.call-update) | async-done | bytes 8388624 | tf_op jit(solution)/shard_map/all_gather | solution.py:26
  415.0 26.3 %while.35 = (s32[]{:T(128)}, f32[1,256,256]{2,1,0:T(8,128)S(1)}, f32[4,256]{1,0:T(4,128)S(1)}, f32[4,256,256]{2,1,0:T(8,128)}, f32[4,256]{1,0:T(4,128)S(1)}, /*i...) while((s32[]{:T(128)}, f32[1,256,256]{2,1,0:T(8,128)S(1)}, ...), condition=%wide.region_14.15_spmd, body=%wide.region_13.14_spmd.sunk | while | flops 329734 | bytes 3956927 | solution.py:35
  415.0 2.7 bitcast_add_fusion.22
  418.7 2.7 bitcast_add_fusion.22
  422.5 2.7 bitcast_add_fusion.22
  426.2 2.7 bitcast_add_fusion.22
  429.9 2.7 bitcast_add_fusion.22
  433.6 2.7 bitcast_add_fusion.22
  437.3 2.7 bitcast_add_fusion.22
  442.0 3.7 fusion.11
  445.8 2.2 fusion.26
  450.0 2.4 fusion.92
  452.4 3.7 fusion.34
  456.1 3.6 fusion.1
  459.7 2.2 fusion
  468.6 2.0 multiply_reduce_fusion
  470.8 3.5 copy.230
  474.3 6.1 %psum.7 = f32[1,3,4]{2,1,0:T(4,128)S(1)} all-reduce(f32[1,3,4]{2,1,0:T(4,128)S(1)} %multiply_bitcast_fusion), channel_id=1, replica_groups=mesh['ctx'=8,'probe'=4] {'probe'}, use_global_device_ids=true, to_apply=%region_17.18 | all-reduce | flops 12 | bytes 96 | tf_op jit(solution)/shard_map/psum | solution.py:140
  (211 shorter events, 42.3 us)
Async XLA Ops:
  7.2 100.4 %all-gather.16.cloned.1.call-start = ((), (), s32[]{:S(2)}) async-start(), calls=%async_computation.1 | async-start | bytes 2359296 | tf_op jit(solution)/shard_map/all_gather | solution.py:26
  11.0 9.8 %copy-start.1 = (f32[1,256,1024]{1,2,0:T(8,128)}, f32[1,256,1024]{1,2,0:T(8,128)S(1)}, u32[]{:S(2)}) copy-start(f32[1,256,1024]{1,2,0:T(8,128)S(1)} %copy.182) | copy-start | bytes 3145732
  13.2 178.2 %all-gather.18.cloned.1.call-start = ((), (), s32[]{:S(2)}) async-start(), calls=%async_computation.2 | async-start | bytes 9437184 | tf_op jit(solution)/shard_map/all_gather | solution.py:26
  24.7 300.1 %all-gather.20.cloned.1.call-start = ((), (), s32[]{:S(2)}) async-start(), calls=%async_computation.3 | async-start | bytes 2359296 | tf_op jit(solution)/shard_map/all_gather | solution.py:26
  24.8 3.4 copy-start.25
  28.1 67.2 %copy-start.6 = (f32[1,256,1024]{1,2,0:T(8,128)}, f32[1,256,1024]{1,2,0:T(8,128)S(1)}, u32[]{:S(2)}) copy-start(f32[1,256,1024]{1,2,0:T(8,128)S(1)} %copy.283) | copy-start | bytes 3145732
  28.2 66.6 %copy-start.60 = (f32[4]{0:T(128)S(1)}, f32[4]{0:T(128)}, u32[]{:S(2)}) copy-start(f32[4]{0:T(128)} %param.10) | copy-start | bytes 52
  95.4 2.5 copy-start.35
  99.8 4.2 copy-start.26
  102.8 121.0 %copy-start.44 = (f32[4,256]{1,0:T(4,128)}, f32[4,256]{1,0:T(4,128)S(1)}, u32[]{:S(2)}) copy-start(f32[4,256]{1,0:T(4,128)S(1)} %get-tuple-element.294) | copy-start | bytes 12292
  102.8 2.6 copy-start.2
  193.3 4.2 copy-start.8
  193.3 8.9 %collective-permute-start = (f32[1,256,256]{1,2,0:T(8,128)}, f32[1,256,256]{1,2,0:T(8,128)S(1)}, u32[]{:S(2)}, u32[]{:S(2)}) collective-permute-start(f32[1,256,256]{1,2,0:T(8,128)} %copy.206), channel_id=1, source_target_pairs={{0,1},{1,2},{2,3},{3,0},{4,5},{5,6},{6,7},{7,4},{8,9},{9,10},{10,1... | collective-permute-start | bytes 786440 | tf_op jit(solution)/shard_map/ppermute | solution.py:15
  193.3 14.8 %collective-permute-start.2 = (f32[1,256,256]{1,2,0:T(8,128)}, f32[1,256,256]{1,2,0:T(8,128)S(1)}, u32[]{:S(2)}, u32[]{:S(2)}) collective-permute-start(f32[1,256,256]{1,2,0:T(8,128)} %copy.206), channel_id=1, source_target_pairs={{0,3},{1,0},{2,1},{3,2},{4,7},{5,4},{6,5},{7,6},{8,11},{9,8},{10,9... | collective-permute-start | bytes 786440 | tf_op jit(solution)/shard_map/ppermute | solution.py:17
  195.5 5.3 %copy-start.23 = (f32[256,4,256]{0,2,1:T(8,128)S(1)}, f32[256,4,256]{0,2,1:T(8,128)}, u32[]{:S(2)}) copy-start(f32[256,4,256]{0,2,1:T(8,128)} %select_add_fusion) | copy-start | bytes 3145732
  200.8 7.3 %copy-start.41 = (f32[1,256,256]{1,2,0:T(8,128)S(1)}, f32[1,256,256]{1,2,0:T(8,128)}, u32[]{:S(2)}) copy-start(f32[1,256,256]{1,2,0:T(8,128)} %copy.206) | copy-start | bytes 786436
  202.2 5.8 %collective-permute-start.1 = (f32[1,256,256]{1,2,0:T(8,128)S(1)}, f32[1,256,256]{1,2,0:T(8,128)S(1)}, u32[]{:S(2)}, u32[]{:S(2)}) collective-permute-start(f32[1,256,256]{1,2,0:T(8,128)S(1)} %collective-permute-done), channel_id=1, source_target_pairs={{0,1},{1,2},{2,3},{3,0},{4,5},{5,6},{6,7},{7,4},{8,9},{9,10},{10,1... | collective-permute-start | bytes 786440 | tf_op jit(solution)/shard_map/ppermute | solution.py:15
  202.3 14.7 %copy-start.48 = (f32[256,4]{0,1:T(4,128)}, f32[256,4]{0,1:T(4,128)S(1)}, u32[]{:S(2)}) copy-start(f32[256,4]{0,1:T(4,128)S(1)} %fusion.107) | copy-start | bytes 12292
  202.3 6.0 %copy-start.53 = (f32[4]{0:T(128)S(1)}, f32[4]{0:T(128)}, u32[]{:S(2)}) copy-start(f32[4]{0:T(128)} %get-tuple-element.336) | copy-start | bytes 52
  212.1 104.8 %copy-start.56 = (f32[256,4]{0,1:T(4,128)}, f32[256,4]{0,1:T(4,128)S(1)}, u32[]{:S(2)}) copy-start(f32[256,4]{0,1:T(4,128)S(1)} %get-tuple-element.352) | copy-start | bytes 12292
  214.4 199.5 %all-gather.22.cloned.1.call-start = ((), (), s32[]{:S(2)}) async-start(), calls=%async_computation.4 | async-start | bytes 9437184 | tf_op jit(solution)/shard_map/all_gather | solution.py:26
  214.4 2.6 copy-start.9
  219.6 236.5 %all-gather.14.cloned.1.call-start = ((), (), s32[]{:S(2)}) async-start(), calls=%async_computation | async-start | bytes 1310720 | tf_op jit(solution)/shard_map/all_gather | solution.py:124
  219.9 2.5 copy-start.3
  219.9 2.5 copy-start.30
  225.2 2.3 copy-start.10
  225.2 3.4 copy-start.24
  227.5 87.3 %copy-start.45 = (f32[4,256]{1,0:T(4,128)S(1)}, f32[4,256]{1,0:T(4,128)}, u32[]{:S(2)}) copy-start(f32[4,256]{1,0:T(4,128)} %copy-done.44) | copy-start | bytes 12292
  227.5 89.4 %copy-start.58 = (f32[4,256]{1,0:T(4,128)}, f32[4,256]{1,0:T(4,128)S(1)}, u32[]{:S(2)}) copy-start(f32[4,256]{1,0:T(4,128)S(1)} %get-tuple-element.349) | copy-start | bytes 12292
  316.9 4.8 copy-start.31
  316.9 2.4 copy-start.16
  319.3 2.4 copy-start.20
  442.0 3.8 copy-start.4
  442.0 3.8 copy-start.37
  442.0 3.8 copy-start.47
  442.0 3.8 copy-start.50
  442.0 3.8 copy-start.52
  445.8 2.2 copy-start.36
  450.0 2.4 copy-start.11
  450.0 2.4 copy-start.40
  450.0 2.4 copy-start.55
  450.0 2.4 copy-start.57
  450.0 2.4 copy-start.59
  452.4 3.7 copy-start.17
  456.1 3.6 copy-start
  459.7 2.2 copy-start.21
  459.7 2.2 copy-start.29
  466.5 2.2 copy-start.43
  (21 other events, 35.4 us)
Sparse Core Ops, SparseCore 0:
  13.3 52.3 all-gather.15
  67.8 123.5 all-gather.17
  214.5 73.7 all-gather.19
  290.3 123.4 all-gather.21
  442.1 13.9 all-gather.13
